TPU v7x, 512 devices: a whole 4x8x8 slice. The times are simulated.
512 devices in a mesh: grp: 8 (over y_lo, core), own: 64 (over x, y_hi, z).
Axes of the slice: x: 4, y: 8 (y_hi: 2, y_lo: 4; y = y_hi * 4 + y_lo), z: 8, core: 2. Of those that a mesh axis runs over, the one named last changes fastest.
Arguments:
- activations: bfloat16 [65536, 1024], P(('grp', 'own'))
- out_grads: bfloat16 [65536, 1024], P(('grp', 'own')), may hold values from -0.01953125 to 0.01953125
- master: float32 [1024, 1024], P('own'), may hold values from -6 to 6
- moment: float32 [1024, 1024], P('own'), may hold values from 0.05 to 5
- left_root: bfloat16 [1024, 1024], P('own'), may hold values from -0.25 to 2.25, as said below
- right_root: bfloat16 [1024, 1024], P('own'), may hold values from -0.25 to 2.25, as said below
- stats_in: float32 [256, 16, 1024], P('own'), may hold values from -6 to 6
- tile_slot: int32 [128], replicated, may hold values from 0 to 255, as said below
Outputs:
- master_out: float32 [1024, 1024], P('own')
- moment_out: float32 [1024, 1024], P('own')
- stats_out: float32 [256, 16, 1024], P('own')
- weights: bfloat16 [1024, 1024], replicated
Inputs may be any that keep to these rules, and one draw needn't show every extreme that they name: `tile_slot`: distinct slot numbers; slot s belongs to owner s // 4; some owner holds 4 tiles. `left_root`: symmetric. `right_root`: symmetric.
All inputs are finite; a program needn't handle non-finite values.
Results may differ from a plain program's by a relative error of at most 0.005.
Values may be sent and summed in bfloat16 or wider, within the bound.
No kernel may reach another device: no remote copies, remote signals or barrier semaphores. Data moves between devices by JAX's collectives and lax.ppermute only.
A program may use at most 64 MiB of HBM per device.

v0:
```python
import jax
import jax.numpy as jnp
from jax import lax
from jax.sharding import PartitionSpec as P

stat_decay = 0.9
moment_decay = 0.95
learn_rate = 0.3
adam_eps = 1e-08
norm_eps = 1e-06


def local(activations, out_grads, master, moment, left_root, right_root, stats_in, tile_slot):
    owner_rows = master.shape[0]
    block_size = master.shape[1]
    capacity = stats_in.shape[0]
    tile_rows = stats_in.shape[1]
    tile_count = tile_slot.shape[0]
    owner_index = lax.axis_index("own")
    gradient = lax.psum(
        lax.dot_general(
            activations, out_grads, (((0,), (0,)), ((), ())), preferred_element_type=jnp.float32
        ),
        ("grp", "own"),
    )
    grad_rows = lax.dynamic_slice_in_dim(gradient, owner_index * owner_rows, owner_rows, 0)
    moment_out = moment_decay * moment + (1.0 - moment_decay) * grad_rows * grad_rows
    adam_dir = grad_rows / (jnp.sqrt(moment_out) + adam_eps)
    my_slots = owner_index * capacity + jnp.arange(capacity, dtype=jnp.int32)
    matches = (tile_slot[:, None] == my_slots[None, :]).astype(jnp.int32)
    tile_ids = jnp.sum(matches * jnp.arange(tile_count, dtype=jnp.int32)[:, None], axis=0)
    filled = jnp.sum(matches, axis=0)
    per_half = block_size // tile_rows

    def slot_update(packed):
        tile_id, slot_filled, old_tile = packed
        which_half = tile_id // per_half
        offset = (tile_id - which_half * per_half) * tile_rows

        def left_product():
            row_block = lax.dynamic_slice_in_dim(gradient, offset, tile_rows, 0)
            return lax.dot_general(
                row_block,
                gradient,
                (((1,), (1,)), ((), ())),
                precision=lax.Precision.HIGHEST,
                preferred_element_type=jnp.float32,
            )

        def right_product():
            column_block = lax.dynamic_slice_in_dim(gradient, offset, tile_rows, 1)
            return lax.dot_general(
                column_block,
                gradient,
                (((0,), (0,)), ((), ())),
                precision=lax.Precision.HIGHEST,
                preferred_element_type=jnp.float32,
            )

        product = lax.cond(which_half == 0, left_product, right_product)
        return jnp.where(
            slot_filled > 0, stat_decay * old_tile + (1.0 - stat_decay) / block_size * product, 0.0
        )

    stats_out = lax.map(slot_update, (tile_ids, filled, stats_in))
    grad_low = gradient.astype(jnp.bfloat16)
    left_mid = jnp.dot(left_root, grad_low, preferred_element_type=jnp.float32).astype(jnp.bfloat16)
    precond = jnp.dot(
        left_mid,
        lax.all_gather(right_root, "own", axis=0, tiled=True),
        preferred_element_type=jnp.float32,
    )
    adam_sum, precond_sum = lax.psum(
        (jnp.sum(adam_dir * adam_dir), jnp.sum(precond * precond)), "own"
    )
    graft_scale = jnp.sqrt(adam_sum) / (jnp.sqrt(precond_sum) + norm_eps)
    master_out = master - learn_rate * graft_scale * precond
    weights = lax.all_gather(master_out.astype(jnp.bfloat16), "own", axis=0, tiled=True)
    return (master_out, moment_out, stats_out, weights)


def solution(mesh):
    in_specs = (
        P(("grp", "own"), None),
        P(("grp", "own"), None),
        P("own", None),
        P("own", None),
        P("own", None),
        P("own", None),
        P("own", None, None),
        P(),
    )
    out_specs = (P("own", None), P("own", None), P("own", None, None), P())
    return jax.shard_map(local, mesh=mesh, in_specs=in_specs, out_specs=out_specs, check_vma=False)
```

profile of v0, /device:TPU:1, one launch (start us, length us, event | category | flops | bytes accessed | tf_op | source)
XLA Modules:
  0.0 681.9 jit_solution(6704430149430638157)
XLA Ops:
  8.0 0.0 copy-start
  8.0 0.0 copy-start.1
  8.0 0.0 copy-start.3
  8.0 0.0 all-reduce.3.cloned.1.call-start
  8.1 0.9 copy-done
  9.0 3.6 fusion.22
  12.6 0.0 all-reduce.3.cloned.1.call-update
  12.6 0.0 copy-start.2
  12.6 0.0 copy-start.4
  12.6 0.0 all-gather.3.cloned.1.call-start
  12.7 0.5 all-gather.3.cloned.1.call-update
  13.2 0.0 all-gather.5.cloned.1.call-start
  13.3 307.7 %all-reduce.3.cloned.1.call-done = f32[1024,1024]{1,0:T(8,128)} async-done(((f32[1024,1024]{1,0:T(8,128)}), f32[1024,1024]{1,0:T(8,128)}) %all-reduce.3.cloned.1.call-update) | async-done | bytes 4194320 | tf_op jit(solution)/shard_map/psum | solution.py:20
  321.0 0.0 copy-done.1
  321.0 2.1 multiply_reduce_fusion.1
  323.1 0.0 all-gather.3.cloned.1.call-done
  323.1 0.0 copy-done.3
  323.1 4.9 multiply_reduce_fusion
  328.0 195.4 %all-reduce = (f32[]{:T(128)}, f32[]{:T(128)}) all-reduce(f32[]{:T(128)} %get-tuple-element.119, f32[]{:T(128)} %get-tuple-element.121), channel_id=1, replica_groups=mesh['grp'=8,'own'=64] {'own'}, use_global_device_ids=true, to_apply=%region_2.0 | all-reduce | flops 2 | bytes 16 | tf_op jit(solution)/shard_map/psum | solution.py:73
  524.8 0.0 copy-done.2
  524.8 0.6 fusion.18
  525.5 0.0 all-gather.5.cloned.1.call-update
  525.5 0.0 copy-done.4
  525.5 0.2 fusion.17
  525.7 50.1 %while.12 = (s32[]{:T(128)}, f32[4,16,1024]{2,1,0:T(8,128)}, s32[4]{0:T(128)S(1)}, f32[4,16,1024]{2,1,0:T(8,128)}, s32[4]{0:T(128)S(1)}, /*index=5*/f32[1024,102...) while((s32[]{:T(128)}, f32[4,16,1024]{2,1,0:T(8,128)}, ...), condition=%wide.region_10.11_spmd, body=%wide.region_7.10_spmd.sunk | while | flops 201392144 | bytes 4982188 | solution.py:65
  525.7 0.7 dynamic_slice.42
  529.9 4.8 conditional.2
  529.9 4.8 fusion
  534.6 0.7 dynamic_slice.43
  536.0 1.5 bitcast_dynamic-update-slice_fusion.2
  537.5 0.7 dynamic_slice.42
  541.6 5.8 conditional.2
  541.6 5.8 fusion.3
  547.4 0.7 dynamic_slice.43
  548.8 1.5 bitcast_dynamic-update-slice_fusion.2
  550.3 0.7 dynamic_slice.42
  554.4 5.8 conditional.2
  554.4 5.8 fusion.3
  560.2 0.7 dynamic_slice.43
  561.6 1.5 bitcast_dynamic-update-slice_fusion.2
  563.1 0.7 dynamic_slice.42
  567.2 5.8 conditional.2
  567.2 5.8 fusion.3
  573.0 0.7 dynamic_slice.43
  574.4 1.5 bitcast_dynamic-update-slice_fusion.2
  575.8 95.5 %all-gather.5.cloned.1.call-done = bf16[1024,1024]{1,0:T(8,128)(2,1)} async-done(((bf16[16,1024]{1,0:T(8,128)(2,1)}), bf16[1024,1024]{1,0:T(8,128)(2,1)}) %all-gather.5.cloned.1.call-update) | async-done | bytes 2097168 | tf_op jit(solution)/shard_map/all_gather | solution.py:78
  671.3 3.1 copy.23
  (2 shorter events, 0.0 us)
Async XLA Ops:
  8.0 1.0 copy-start
  8.0 313.0 %copy-start.1 = (f32[16,1024]{1,0:T(8,128)S(1)}, f32[16,1024]{1,0:T(8,128)}, u32[]{:S(2)}) copy-start(f32[16,1024]{1,0:T(8,128)} %param.15) | copy-start | bytes 196612
  8.0 315.1 %copy-start.3 = (bf16[16,1024]{1,0:T(8,128)(2,1)S(1)}, bf16[16,1024]{1,0:T(8,128)(2,1)}, u32[]{:S(2)}) copy-start(bf16[16,1024]{1,0:T(8,128)(2,1)} %param.16) | copy-start | bytes 98308
  8.0 312.9 %all-reduce.3.cloned.1.call-start = ((), (), s32[]{:S(2)}) async-start(), calls=%async_computation | async-start | bytes 8388608 | tf_op jit(solution)/shard_map/psum | solution.py:20
  12.6 512.2 %copy-start.2 = (f32[16,1024]{1,0:T(8,128)S(1)}, f32[16,1024]{1,0:T(8,128)}, u32[]{:S(2)}) copy-start(f32[16,1024]{1,0:T(8,128)} %param.14) | copy-start | bytes 196612
  12.6 512.9 %copy-start.4 = (s32[128]{0:T(128)S(1)}, s32[128]{0:T(128)}, u32[]{:S(2)}) copy-start(s32[128]{0:T(128)} %param.19) | copy-start | bytes 1540
  12.6 310.4 %all-gather.3.cloned.1.call-start = ((), (), s32[]{:S(2)}) async-start(), calls=%async_computation.1 | async-start | bytes 2129920 | tf_op jit(solution)/shard_map/all_gather | solution.py:70
  13.2 658.1 %all-gather.5.cloned.1.call-start = ((), (), s32[]{:S(2)}) async-start(), calls=%async_computation.2 | async-start | bytes 2129920 | tf_op jit(solution)/shard_map/all_gather | solution.py:78
Sparse Core Ops, SparseCore 0:
  13.8 307.1 all-reduce.2
Sparse Core Ops, SparseCore 1:
  17.7 135.7 all-gather.2
  525.6 145.7 all-gather.4
where the time goes:
time: 688 us; the launch traced here: 682 us
  waiting for transfers between devices  404 us (59%)
  blocking collectives  195 us (28%)
  matrix products  30.6 us (4%)
  between operations  17 us (2%)
  loops' own time  16.8 us (2%)
  local copies, waits for them, and re-layouts  9.33 us (1%)
  other arithmetic  8.89 us (1%)
    psum x1, waiting for transfers between devices, local(): lax.psum(lax.dot_general(activations, out_grads, (((0,), (0,)), ((), ()))...  308 us
    psum x1, blocking collectives, local(): lax.psum((jnp.sum(adam_dir * adam_dir), jnp.sum(precond * precond)), 'own')  195 us
    all_gather x1, waiting for transfers between devices, local(): lax.all_gather(master_out.astype(jnp.bfloat16), 'own', axis=0, tiled=True)  95.5 us
    dot_general x3, matrix products, left_product(): lax.dot_general(row_block, gradient, (((1,), (1,)), ((), ())), precision=...  17.3 us
    another operation x1, loops' own time, local(): stats_out = lax.map(slot_update, (tile_ids, filled, stats_in))  16.7 us
  transfers between devices with their start and end apart: 3, of which 2 were waited for; matrix products, arithmetic and copies ran while one was open for 5% of the time, Pallas kernels for 0%

commit v1 on v0

v1 whole, which is shorter than its diff:
```python
import jax
import jax.numpy as jnp
from jax import lax
from jax.sharding import Mesh
from jax.sharding import PartitionSpec as P

stat_decay = 0.9
moment_decay = 0.95
learn_rate = 0.3
adam_eps = 1e-08
norm_eps = 1e-06

GRP = ("yl", "c")
OWN = ("x", "yh", "z")
SUB_SIZES = (4, 2, 4, 2, 8)


def split3(value):
    hi = lax.reduce_precision(value, exponent_bits=8, mantissa_bits=7)
    rest = value - hi
    mid = lax.reduce_precision(rest, exponent_bits=8, mantissa_bits=7)
    lo = lax.reduce_precision(rest - mid, exponent_bits=8, mantissa_bits=7)
    return jnp.stack([hi, mid, lo])


def gather_own_rows(block):
    rows = block.shape[0]
    out = block
    for axis in ("yh", "x", "z"):
        out = lax.all_gather(out, axis, axis=0, tiled=True)
    out = out.reshape(SUB_SIZES[4], SUB_SIZES[2], SUB_SIZES[3], rows, block.shape[1])
    out = jnp.transpose(out, (1, 2, 0, 3, 4))
    return out.reshape(-1, block.shape[1])


def local(activations, out_grads, master, moment, left_root, right_root, stats_in, tile_slot):
    owner_rows = master.shape[0]
    block_size = master.shape[1]
    owners = block_size // owner_rows
    capacity = stats_in.shape[0]
    tile_rows = stats_in.shape[1]
    tile_count = tile_slot.shape[0]
    owner_index = lax.axis_index(OWN)
    grp_size = SUB_SIZES[0] * SUB_SIZES[1]

    left_full = gather_own_rows(left_root)
    right_full = gather_own_rows(right_root)
    master_full = gather_own_rows(master)

    partial = lax.dot_general(
        activations, out_grads, (((0,), (0,)), ((), ())), preferred_element_type=jnp.float32
    )
    pieces = lax.all_to_all(
        partial.reshape(owners, owner_rows, block_size), OWN, 0, 0, tiled=True
    )
    own_sum = jnp.sum(pieces, axis=0)
    copies = jnp.broadcast_to(own_sum[None], (grp_size, owner_rows, block_size))
    grad_rows = jnp.sum(lax.all_to_all(copies, GRP, 0, 0, tiled=True), axis=0)

    moment_out = moment_decay * moment + (1.0 - moment_decay) * grad_rows * grad_rows
    adam_dir = grad_rows / (jnp.sqrt(moment_out) + adam_eps)
    adam_part = split3(jnp.sum(adam_dir * adam_dir))

    extra = jnp.zeros((1, block_size), jnp.float32).at[0, :3].set(adam_part)
    payload = jnp.concatenate([grad_rows, extra], axis=0).astype(jnp.bfloat16)
    sent = jnp.broadcast_to(payload[None], (owners,) + payload.shape)
    got = lax.all_to_all(sent, OWN, 0, 0, tiled=True)
    grad_low = got[:, :owner_rows, :].reshape(block_size, block_size)
    adam_sum = jnp.sum(got[:, owner_rows, :3].astype(jnp.float32))

    left_mid = jnp.dot(left_full, grad_low, preferred_element_type=jnp.float32).astype(jnp.bfloat16)
    precond = jnp.dot(left_mid, right_full, preferred_element_type=jnp.float32)
    graft_scale = jnp.sqrt(adam_sum) / (jnp.sqrt(jnp.sum(precond * precond)) + norm_eps)
    master_out_full = master_full - learn_rate * graft_scale * precond
    weights = master_out_full.astype(jnp.bfloat16)
    master_out = lax.dynamic_slice_in_dim(master_out_full, owner_index * owner_rows, owner_rows, 0)

    my_slots = owner_index * capacity + jnp.arange(capacity, dtype=jnp.int32)
    matches = (tile_slot[:, None] == my_slots[None, :]).astype(jnp.int32)
    tile_ids = jnp.sum(matches * jnp.arange(tile_count, dtype=jnp.int32)[:, None], axis=0)
    filled = jnp.sum(matches, axis=0)
    per_half = block_size // tile_rows
    which_half = tile_ids // per_half
    offsets = (tile_ids - which_half * per_half) * tile_rows
    grad_low_t = grad_low.T
    row_blocks = jnp.concatenate(
        [lax.dynamic_slice_in_dim(grad_low, offsets[s], tile_rows, 0) for s in range(capacity)], axis=0
    )
    col_blocks = jnp.concatenate(
        [lax.dynamic_slice_in_dim(grad_low_t, offsets[s], tile_rows, 0) for s in range(capacity)], axis=0
    )
    left_tiles = lax.dot_general(
        row_blocks, grad_low, (((1,), (1,)), ((), ())), preferred_element_type=jnp.float32
    ).reshape(capacity, tile_rows, block_size)
    right_tiles = jnp.dot(col_blocks, grad_low, preferred_element_type=jnp.float32).reshape(
        capacity, tile_rows, block_size
    )
    product = jnp.where((which_half == 0)[:, None, None], left_tiles, right_tiles)
    fresh = stat_decay * stats_in + (1.0 - stat_decay) / block_size * product
    stats_out = jnp.where((filled > 0)[:, None, None], fresh, 0.0)
    return (master_out, moment_out, stats_out, weights)


def solution(mesh):
    sub_mesh = Mesh(mesh.devices.reshape(SUB_SIZES), GRP + OWN)
    rows_all = P(GRP + OWN, None)
    rows_own = P(OWN, None)
    in_specs = (rows_all, rows_all, rows_own, rows_own, rows_own, rows_own, P(OWN, None, None), P())
    out_specs = (rows_own, rows_own, P(OWN, None, None), P())
    return jax.shard_map(local, mesh=sub_mesh, in_specs=in_specs, out_specs=out_specs, check_vma=False)
```

time: 688 us -> 374 us (0.54)
  waiting for transfers between devices: 404 us -> 100 us
  starting transfers between devices: 0.12 us -> 48.8 us
  blocking collectives: 195 us -> 148 us
  loops' own time: 16.8 us -> 0 us
  matrix products: 30.6 us -> 15 us
  between operations: 17 us -> 27.2 us
  local copies, waits for them, and re-layouts: 9.33 us -> 17.9 us
    psum x1 -> x0, waiting for transfers between devices: 308 us -> none  [local(): lax.psum(lax.dot_general(activations, out_grads, (((0,), (0,)), ((), ()))...]
    psum x1 -> x0, blocking collectives: 195 us -> none  [local(): lax.psum((jnp.sum(adam_dir * adam_dir), jnp.sum(precond * precond)), 'own')]
    all_gather x0 -> x6, blocking collectives: none -> 148 us  [gather_own_rows(): out = lax.all_gather(out, axis, axis=0, tiled=True)]
    all_to_all x0 -> x3, starting transfers between devices: none -> 48.7 us  [the longest x1 18.3 us: local(): lax.all_to_all(partial.reshape(owners, owner_rows, block_size), OWN, 0, 0...]
    another operation x5 -> x0, loops' own time: 16.8 us -> none  [the longest x1 16.7 us: local(): stats_out = lax.map(slot_update, (tile_ids, filled, stats_in))]
    dot_general x5 -> x3, matrix products: 27 us -> 11.4 us  [the longest x1 9.43 us: local(): precond = jnp.dot(left_mid, right_full, preferred_element_type=jnp.float32)]
    all_to_all x0 -> x3, waiting for transfers between devices: none -> 13.7 us  [the longest x1 13.7 us: local(): grad_rows = jnp.sum(lax.all_to_all(copies, GRP, 0, 0, tiled=True), axis=0)]
    all_gather x2 -> x3, waiting for transfers between devices: 95.5 us -> 86.7 us  [gather_own_rows(): out = lax.all_gather(out, axis, axis=0, tiled=True)]
  transfers between devices with their start and end apart: 3 -> 6, of which waited for: 2 -> 2; matrix products, arithmetic and copies ran while one was open for 5% -> 7% of each run, Pallas kernels for 0% -> 0%
where the time goes in v1:
time: 374 us; the launch traced here: 373 us
  blocking collectives  148 us (40%)
  waiting for transfers between devices  100 us (27%)
  starting transfers between devices  48.8 us (13%)
  between operations  27.2 us (7%)
  local copies, waits for them, and re-layouts  17.9 us (5%)
  other arithmetic  15.5 us (4%)
  matrix products  15 us (4%)
    all_gather x6, blocking collectives, gather_own_rows(): out = lax.all_gather(out, axis, axis=0, tiled=True)  148 us
    all_gather x3, waiting for transfers between devices, gather_own_rows(): out = lax.all_gather(out, axis, axis=0, tiled=True)  86.7 us
    all_to_all x1, starting transfers between devices, local(): lax.all_to_all(partial.reshape(owners, owner_rows, block_size), OWN, 0, 0...  18.3 us
    all_to_all x1, starting transfers between devices, local(): grad_rows = jnp.sum(lax.all_to_all(copies, GRP, 0, 0, tiled=True), axis=0)  16.6 us
    all_to_all x1, starting transfers between devices, local(): got = lax.all_to_all(sent, OWN, 0, 0, tiled=True)  13.8 us
    all_to_all x1, waiting for transfers between devices, local(): grad_rows = jnp.sum(lax.all_to_all(copies, GRP, 0, 0, tiled=True), axis=0)  13.7 us
    dot_general x1, matrix products, local(): precond = jnp.dot(left_mid, right_full, preferred_element_type=jnp.float32)  9.43 us
  transfers between devices with their start and end apart: 6, of which 2 were waited for; matrix products, arithmetic and copies ran while one was open for 7% of the time, Pallas kernels for 0%

profile of v1, /device:TPU:1, one launch (start us, length us, event | category | flops | bytes accessed | tf_op | source)
XLA Modules:
  0.0 372.7 jit_solution(11334056759596255519)
XLA Ops:
  7.2 0.0 copy-start
  7.2 0.0 all-gather.6.cloned.1.call-start
  7.2 8.8 %all_gather.30 = bf16[32,1024]{1,0:T(8,128)(2,1)S(1)} all-gather(bf16[16,1024]{1,0:T(8,128)(2,1)} %param.14), channel_id=1, replica_groups=mesh['yl'=4,'c'=2,'x'=4,'yh'=2,'z'=8] {'yh'}, dimensions={0}, use_global_device_ids=true | all-gather | bytes 98304 | tf_op jit(solution)/shard_map/all_gather | solution.py:30
  16.1 10.6 %all_gather.31 = bf16[128,1024]{1,0:T(8,128)(2,1)} all-gather(bf16[32,1024]{1,0:T(8,128)(2,1)S(1)} %all_gather.30), channel_id=1, replica_groups=mesh['yl'=4,'c'=2,'x'=4,'yh'=2,'z'=8] {'x'}, dimensions={0}, use_global_device_ids=true | all-gather | bytes 327680 | tf_op jit(solution)/shard_map/all_gather | solution.py:30
  26.7 0.0 all-gather.6.cloned.1.call-update
  26.7 0.0 copy-done
  26.7 3.6 fusion.15
  30.4 18.3 %all-to-all-start = ((f32[64,16,1024]{2,1,0:T(8,128)}), f32[64,16,1024]{2,1,0:T(8,128)}, u32[]{:S(2)}, u32[]{:S(2)}) async-start(f32[64,16,1024]{2,1,0:T(8,128)} %bitcast.51), calls=%async_computation | async-start | bytes 8388608 | tf_op jit(solution)/shard_map/all_to_all | solution.py:53
  48.7 0.0 all-gather.8.cloned.1.call-start
  48.7 93.9 %all_gather.33 = bf16[32,1024]{1,0:T(8,128)(2,1)S(1)} all-gather(bf16[16,1024]{1,0:T(8,128)(2,1)S(1)} %copy-done.4), channel_id=1, replica_groups=mesh['yl'=4,'c'=2,'x'=4,'yh'=2,'z'=8] {'yh'}, dimensions={0}, use_global_device_ids=true | all-gather | bytes 98304 | tf_op jit(solution)/shard_map/all_gather | solution.py:30
  142.6 15.0 %all_gather.34 = bf16[128,1024]{1,0:T(8,128)(2,1)} all-gather(bf16[32,1024]{1,0:T(8,128)(2,1)S(1)} %all_gather.33), channel_id=1, replica_groups=mesh['yl'=4,'c'=2,'x'=4,'yh'=2,'z'=8] {'x'}, dimensions={0}, use_global_device_ids=true | all-gather | bytes 327680 | tf_op jit(solution)/shard_map/all_gather | solution.py:30
  157.6 0.0 all-gather.8.cloned.1.call-update
  157.6 0.0 all-gather.4.cloned.1.call-start
  157.7 0.0 copy-done.2
  157.7 7.7 %all_gather.27 = f32[32,1024]{1,0:T(8,128)S(1)} all-gather(f32[16,1024]{1,0:T(8,128)S(1)} %copy-done.2), channel_id=1, replica_groups=mesh['yl'=4,'c'=2,'x'=4,'yh'=2,'z'=8] {'yh'}, dimensions={0}, use_global_device_ids=true | all-gather | bytes 196608 | tf_op jit(solution)/shard_map/all_gather | solution.py:30
  165.4 11.8 %all_gather.28 = f32[128,1024]{1,0:T(8,128)} all-gather(f32[32,1024]{1,0:T(8,128)S(1)} %all_gather.27), channel_id=1, replica_groups=mesh['yl'=4,'c'=2,'x'=4,'yh'=2,'z'=8] {'x'}, dimensions={0}, use_global_device_ids=true | all-gather | bytes 655360 | tf_op jit(solution)/shard_map/all_gather | solution.py:30
  177.2 0.0 all-gather.4.cloned.1.call-update
  177.2 0.0 all-to-all-done
  177.2 2.4 reduce_sum.63
  179.6 0.0 copy-start.3
  179.6 0.8 broadcast_in_dim.20
  180.5 16.6 %all-to-all-start.1 = ((f32[8,16,1024]{2,1,0:T(8,128)}), f32[8,16,1024]{2,1,0:T(8,128)S(1)}, u32[]{:S(2)}, u32[]{:S(2)}) async-start(f32[8,16,1024]{2,1,0:T(8,128)} %broadcast_in_dim.20), calls=%async_computation.1 | async-start | bytes 1048576 | tf_op jit(solution)/shard_map/all_to_all | solution.py:58
  197.1 0.6 compare_reduce_fusion
  197.7 13.7 %all-to-all-done.1 = f32[8,16,1024]{2,1,0:T(8,128)S(1)} async-done(((f32[8,16,1024]{2,1,0:T(8,128)}), f32[8,16,1024]{2,1,0:T(8,128)S(1)}, u32[]{:S(2)}, u32[]{:S(2)}) %all-to-all-start.1) | async-done | bytes 524320 | tf_op jit(solution)/shard_map/all_to_all | solution.py:58
  211.5 1.3 multiply_reduce_fusion.1
  216.9 2.6 fusion.11
  219.5 2.1 broadcast_in_dim.21
  221.7 13.8 %all-to-all-start.2 = ((bf16[64,17,1024]{2,1,0:T(8,128)(2,1)}), bf16[64,17,1024]{2,1,0:T(8,128)(2,1)}, u32[]{:S(2)}, u32[]{:S(2)}) async-start(bf16[64,17,1024]{2,1,0:T(8,128)(2,1)} %broadcast_in_dim.21), calls=%async_computation.2 | async-start | bytes 6291456 | tf_op jit(solution)/shard_map/all_to_all | solution.py:67
  235.5 0.2 fusion.9
  235.7 0.6 fusion.14
  244.1 0.0 all-gather.6.cloned.1.call-done
  244.1 3.2 copy.21
  247.3 3.3 copy.22
  250.6 86.7 %all-gather.4.cloned.1.call-done = f32[1024,1024]{1,0:T(8,128)} async-done(((f32[128,1024]{1,0:T(8,128)}), f32[1024,1024]{1,0:T(8,128)}) %all-gather.4.cloned.1.call-update) | async-done | bytes 4194320 | tf_op jit(solution)/shard_map/all_gather | solution.py:30
  337.2 4.8 %copy.20 = f32[8,4,2,16,1024]{4,3,0,2,1:T(8,128)} copy(f32[8,4,2,16,1024]{4,3,2,1,0:T(8,128)} %bitcast.52) | data formatting | bytes 8388608 | tf_op jit(solution)/shard_map/reshape | solution.py:31
  342.0 0.0 all-to-all-done.2
  342.0 1.8 slice.45
  343.8 0.4 dynamic-slice_bitcast_fusion.3
  344.2 0.1 constant_dynamic-slice_fusion.3
  344.3 0.4 pad_maximum_fusion
  344.7 0.1 copy.23
  344.8 9.4 %multiply_reduce_fusion = (f32[]{:T(128)}, f32[1024,1024]{1,0:T(8,128)}) fusion(bf16[1024,1024]{1,0:T(8,128)(2,1)} %bitcast.56, bf16[1024,1024]{1,0:T(8,128)(2,1)S(1)} %bitcast.48, bf16[1024,1024]{1,0:T(8,128)(2,1)} %bitcast.55), kind=kOutput, calls=%fused_computation.1 | convolution fusion | flops 4298113024 | bytes 10485764 | tf_op jit(solution)/shard_map/dot_general | solution.py:72
  354.9 1.6 fusion.8
  357.2 0.8 fusion.16
  358.0 0.0 copy-start.1
  358.0 6.3 %fusion.12 = (bf16[1024,1024]{1,0:T(8,128)(2,1)}, f32[1024,1024]{1,0:T(8,128)S(1)}) fusion(f32[1024,1024]{1,0:T(8,128)} %get-tuple-element.38, f32[]{:T(128)S(6)} %mul_shard_map.3, f32[8,4,2,16,1024]{4,3,0,2,1:T(8,128)} %copy.20), kind=kLoop, calls=%fused_computation.42 | loop fusion | flops 3145728 | bytes 14680068 | tf_op jit(solution)/shard_map/convert_element_type | solution.py:75
  364.3 0.6 constant_dynamic-slice_fusion.4
  365.0 1.2 fusion.4
  (16 shorter events, 0.1 us)
Async XLA Ops:
  7.2 19.6 %copy-start = (bf16[128,1024]{1,0:T(8,128)(2,1)S(1)}, bf16[128,1024]{1,0:T(8,128)(2,1)}, u32[]{:S(2)}) copy-start(bf16[128,1024]{1,0:T(8,128)(2,1)} %param.10) | copy-start | bytes 786436
  7.2 236.9 %all-gather.6.cloned.1.call-start = ((), (), s32[]{:S(2)}) async-start(), calls=%async_computation.4 | async-start | bytes 2359296 | tf_op jit(solution)/shard_map/all_gather | solution.py:30
  30.4 18.4 %copy-start.4 = (bf16[16,1024]{1,0:T(8,128)(2,1)S(1)}, bf16[16,1024]{1,0:T(8,128)(2,1)}, u32[]{:S(2)}) copy-start(bf16[16,1024]{1,0:T(8,128)(2,1)} %param.15) | copy-start | bytes 98308
  30.4 127.3 %copy-start.2 = (f32[16,1024]{1,0:T(8,128)S(1)}, f32[16,1024]{1,0:T(8,128)}, u32[]{:S(2)}) copy-start(f32[16,1024]{1,0:T(8,128)} %param.12) | copy-start | bytes 196612
  30.4 146.8 %all-to-all-start = ((f32[64,16,1024]{2,1,0:T(8,128)}), f32[64,16,1024]{2,1,0:T(8,128)}, u32[]{:S(2)}, u32[]{:S(2)}) async-start(f32[64,16,1024]{2,1,0:T(8,128)} %bitcast.51), calls=%async_computation | async-start | bytes 8388608 | tf_op jit(solution)/shard_map/all_to_all | solution.py:53
  48.7 198.6 %all-gather.8.cloned.1.call-start = ((), (), s32[]{:S(2)}) async-start(), calls=%async_computation.5 | async-start | bytes 2359296 | tf_op jit(solution)/shard_map/all_gather | solution.py:30
  157.6 179.6 %all-gather.4.cloned.1.call-start = ((), (), s32[]{:S(2)}) async-start(), calls=%async_computation.3 | async-start | bytes 4718592 | tf_op jit(solution)/shard_map/all_gather | solution.py:30
  179.6 31.8 %copy-start.3 = (f32[16,1024]{1,0:T(8,128)S(1)}, f32[16,1024]{1,0:T(8,128)}, u32[]{:S(2)}) copy-start(f32[16,1024]{1,0:T(8,128)} %param.13) | copy-start | bytes 196612
  180.5 30.9 %all-to-all-start.1 = ((f32[8,16,1024]{2,1,0:T(8,128)}), f32[8,16,1024]{2,1,0:T(8,128)S(1)}, u32[]{:S(2)}, u32[]{:S(2)}) async-start(f32[8,16,1024]{2,1,0:T(8,128)} %broadcast_in_dim.20), calls=%async_computation.1 | async-start | bytes 1048576 | tf_op jit(solution)/shard_map/all_to_all | solution.py:58
  221.7 13.8 %copy-start.5 = (s32[128]{0:T(128)S(1)}, s32[128]{0:T(128)}, u32[]{:S(2)}) copy-start(s32[128]{0:T(128)} %param.17) | copy-start | bytes 1540
  221.7 120.3 %all-to-all-start.2 = ((bf16[64,17,1024]{2,1,0:T(8,128)(2,1)}), bf16[64,17,1024]{2,1,0:T(8,128)(2,1)}, u32[]{:S(2)}, u32[]{:S(2)}) async-start(bf16[64,17,1024]{2,1,0:T(8,128)(2,1)} %broadcast_in_dim.21), calls=%async_computation.2 | async-start | bytes 6291456 | tf_op jit(solution)/shard_map/all_to_all | solution.py:67
  358.0 7.0 %copy-start.1 = (f32[4,16,1024]{2,1,0:T(8,128)S(1)}, f32[4,16,1024]{2,1,0:T(8,128)}, u32[]{:S(2)}) copy-start(f32[4,16,1024]{2,1,0:T(8,128)} %param.16) | copy-start | bytes 786436
Sparse Core Ops, SparseCore 0:
  26.8 132.8 all-gather.5
  161.9 45.4 all-gather.7
  209.4 127.7 all-gather.3

commit v2 on v1

--- a/solution.py
+++ b/solution.py
@@ -43,9 +43,7 @@
     owner_index = lax.axis_index(OWN)
     grp_size = SUB_SIZES[0] * SUB_SIZES[1]
 
-    left_full = gather_own_rows(left_root)
     right_full = gather_own_rows(right_root)
-    master_full = gather_own_rows(master)
 
     partial = lax.dot_general(
         activations, out_grads, (((0,), (0,)), ((), ())), preferred_element_type=jnp.float32
@@ -68,12 +66,14 @@
     grad_low = got[:, :owner_rows, :].reshape(block_size, block_size)
     adam_sum = jnp.sum(got[:, owner_rows, :3].astype(jnp.float32))
 
-    left_mid = jnp.dot(left_full, grad_low, preferred_element_type=jnp.float32).astype(jnp.bfloat16)
+    left_mid = jnp.dot(left_root, grad_low, preferred_element_type=jnp.float32).astype(jnp.bfloat16)
     precond = jnp.dot(left_mid, right_full, preferred_element_type=jnp.float32)
-    graft_scale = jnp.sqrt(adam_sum) / (jnp.sqrt(jnp.sum(precond * precond)) + norm_eps)
-    master_out_full = master_full - learn_rate * graft_scale * precond
-    weights = master_out_full.astype(jnp.bfloat16)
-    master_out = lax.dynamic_slice_in_dim(master_out_full, owner_index * owner_rows, owner_rows, 0)
+    precond_part = jnp.broadcast_to(jnp.sum(precond * precond), (owners, 1, 128))
+    precond_sum = jnp.sum(lax.all_to_all(precond_part, OWN, 0, 0, tiled=True)[:, 0, 0])
+    graft_scale = jnp.sqrt(adam_sum) / (jnp.sqrt(precond_sum) + norm_eps)
+    master_out = master - learn_rate * graft_scale * precond
+    weight_rows = jnp.broadcast_to(master_out.astype(jnp.bfloat16)[None], (owners, owner_rows, block_size))
+    weights = lax.all_to_all(weight_rows, OWN, 0, 0, tiled=True).reshape(block_size, block_size)
 
     my_slots = owner_index * capacity + jnp.arange(capacity, dtype=jnp.int32)
     matches = (tile_slot[:, None] == my_slots[None, :]).astype(jnp.int32)

time: 374 us -> 409 us (1.094)
  the two profiles are of different devices: /device:TPU:1 before, /device:TPU:8 now
where the time goes in v2:
time: 409 us; the launch traced here: 408 us
  blocking collectives  196 us (48%)
  waiting for transfers between devices  124 us (30%)
  starting transfers between devices  27.8 us (7%)
  between operations  27.3 us (7%)
  local copies, waits for them, and re-layouts  16.2 us (4%)
  other arithmetic  10.5 us (3%)
  matrix products  6.56 us (2%)
    all_to_all x1, blocking collectives, local(): lax.all_to_all(partial.reshape(owners, owner_rows, block_size), OWN, 0, 0...  123 us
    all_gather x2, blocking collectives, gather_own_rows(): out = lax.all_gather(out, axis, axis=0, tiled=True)  73 us
    all_gather x1, waiting for transfers between devices, gather_own_rows(): out = lax.all_gather(out, axis, axis=0, tiled=True)  58.9 us
    all_to_all x1, waiting for transfers between devices, local(): lax.all_to_all(weight_rows, OWN, 0, 0, tiled=True)  41.4 us
    all_to_all x1, waiting for transfers between devices, local(): lax.all_to_all(precond_part, OWN, 0, 0, tiled=True)[:, 0, 0]  12 us
    all_to_all x1, starting transfers between devices, local(): lax.all_to_all(precond_part, OWN, 0, 0, tiled=True)[:, 0, 0]  11.8 us
    all_to_all x1, waiting for transfers between devices, local(): grad_rows = jnp.sum(lax.all_to_all(copies, GRP, 0, 0, tiled=True), axis=0)  11.3 us
  transfers between devices with their start and end apart: 5, of which 4 were waited for; matrix products, arithmetic and copies ran while one was open for 2% of the time, Pallas kernels for 0%

profile of v2, /device:TPU:8, one launch (start us, length us, event | category | flops | bytes accessed | tf_op | source)
XLA Modules:
  0.0 407.6 jit_solution(5947708179712578350)
XLA Ops:
  7.2 0.0 copy-start
  7.2 0.9 copy-done
  8.1 1.7 fusion.12
  9.8 122.6 %all_to_all.25 = f32[64,16,1024]{2,1,0:T(8,128)} all-to-all(f32[64,16,1024]{2,1,0:T(8,128)S(1)} %bitcast.42), channel_id=1, replica_groups=mesh['yl'=4,'c'=2,'x'=4,'yh'=2,'z'=8] {'x','yh','z'}, dimensions={0} | all-to-all | bytes 8388608 | tf_op jit(solution)/shard_map/all_to_all | solution.py:51
  132.4 2.4 reduce_sum.72
  134.8 0.0 copy-start.2
  134.8 0.8 broadcast_in_dim.24
  135.6 3.4 all-to-all-start.1
  139.1 0.6 compare_reduce_fusion
  139.7 11.3 %all-to-all-done.1 = f32[8,16,1024]{2,1,0:T(8,128)S(1)} async-done(((f32[8,16,1024]{2,1,0:T(8,128)}), f32[8,16,1024]{2,1,0:T(8,128)S(1)}, u32[]{:S(2)}, u32[]{:S(2)}) %all-to-all-start.1) | async-done | bytes 524320 | tf_op jit(solution)/shard_map/all_to_all | solution.py:56
  151.1 0.0 copy-done.2
  151.1 1.3 multiply_reduce_fusion.1
  156.5 2.7 fusion.8
  159.3 2.1 broadcast_in_dim.25
  161.4 6.8 %all-to-all-start.2 = ((bf16[64,17,1024]{2,1,0:T(8,128)(2,1)}), bf16[64,17,1024]{2,1,0:T(8,128)(2,1)}, u32[]{:S(2)}, u32[]{:S(2)}) async-start(bf16[64,17,1024]{2,1,0:T(8,128)(2,1)} %broadcast_in_dim.25), calls=%async_computation.2 | async-start | bytes 6291456 | tf_op jit(solution)/shard_map/all_to_all | solution.py:65
  168.2 0.0 all-gather.2.cloned.1.call-start
  168.3 0.0 copy-done.5
  168.3 53.6 %all_gather.9 = bf16[32,1024]{1,0:T(8,128)(2,1)S(1)} all-gather(bf16[16,1024]{1,0:T(8,128)(2,1)S(1)} %copy-done.5), channel_id=1, replica_groups=mesh['yl'=4,'c'=2,'x'=4,'yh'=2,'z'=8] {'yh'}, dimensions={0}, use_global_device_ids=true | all-gather | bytes 98304 | tf_op jit(solution)/shard_map/all_gather | solution.py:30
  221.9 19.4 %all_gather.10 = bf16[128,1024]{1,0:T(8,128)(2,1)} all-gather(bf16[32,1024]{1,0:T(8,128)(2,1)S(1)} %all_gather.9), channel_id=1, replica_groups=mesh['yl'=4,'c'=2,'x'=4,'yh'=2,'z'=8] {'x'}, dimensions={0}, use_global_device_ids=true | all-gather | bytes 327680 | tf_op jit(solution)/shard_map/all_gather | solution.py:30
  241.3 0.0 all-gather.2.cloned.1.call-update
  241.3 58.9 %all-gather.2.cloned.1.call-done = bf16[1024,1024]{1,0:T(8,128)(2,1)} async-done(((bf16[128,1024]{1,0:T(8,128)(2,1)}), bf16[1024,1024]{1,0:T(8,128)(2,1)}) %all-gather.2.cloned.1.call-update) | async-done | bytes 2097168 | tf_op jit(solution)/shard_map/all_gather | solution.py:30
  300.2 3.2 copy.18
  303.4 0.0 all-to-all-done.2
  303.4 1.9 slice.49
  305.3 0.0 copy-done.4
  305.3 0.0 copy-start.3
  305.3 2.9 multiply_reduce_fusion
  308.2 1.3 broadcast_in_dim.26
  309.5 11.8 %all-to-all-start.3 = ((f32[64,1,128]{2,1,0:T(1,128)}), f32[64,1,128]{2,1,0:T(1,128)S(1)}, u32[]{:S(2)}, u32[]{:S(2)}) async-start(f32[64,1,128]{2,1,0:T(1,128)} %broadcast_in_dim.26), calls=%async_computation.3 | async-start | bytes 65536 | tf_op jit(solution)/shard_map/all_to_all | solution.py:72
  321.3 1.6 fusion.5
  323.6 12.0 %all-to-all-done.3 = f32[64,1,128]{2,1,0:T(1,128)S(1)} async-done(((f32[64,1,128]{2,1,0:T(1,128)}), f32[64,1,128]{2,1,0:T(1,128)S(1)}, u32[]{:S(2)}, u32[]{:S(2)}) %all-to-all-start.3) | async-done | bytes 32800 | tf_op jit(solution)/shard_map/all_to_all | solution.py:72
  335.5 0.7 slice_reduce_fusion
  336.9 0.0 copy-done.3
  337.0 0.6 fusion.9
  337.6 1.6 broadcast_in_dim.53
  339.2 5.7 %all-to-all-start.4 = ((bf16[64,16,1024]{2,1,0:T(8,128)(2,1)}), bf16[64,16,1024]{2,1,0:T(8,128)(2,1)}, u32[]{:S(2)}, u32[]{:S(2)}) async-start(bf16[64,16,1024]{2,1,0:T(8,128)(2,1)} %broadcast_in_dim.53), calls=%async_computation.4 | async-start | bytes 4194304 | tf_op jit(solution)/shard_map/all_to_all | solution.py:76
  344.9 0.0 copy-done.6
  344.9 0.2 fusion.6
  345.1 0.6 fusion.11
  353.2 0.4 dynamic-slice_bitcast_fusion.3
  353.7 0.0 copy-start.1
  353.7 0.4 pad_maximum_fusion
  354.0 0.1 copy.20
  354.2 0.1 constant_dynamic-slice_fusion.3
  354.2 0.8 fusion.13
  355.0 1.2 fusion.2
  356.2 41.4 %all-to-all-done.4 = bf16[64,16,1024]{2,1,0:T(8,128)(2,1)} async-done(((bf16[64,16,1024]{2,1,0:T(8,128)(2,1)}), bf16[64,16,1024]{2,1,0:T(8,128)(2,1)}, u32[]{:S(2)}, u32[]{:S(2)}) %all-to-all-start.4) | async-done | bytes 2097184 | tf_op jit(solution)/shard_map/all_to_all | solution.py:76
  397.7 3.1 copy.23
  (12 shorter events, 0.1 us)
Async XLA Ops:
  7.2 1.0 copy-start
  134.8 16.3 %copy-start.2 = (f32[16,1024]{1,0:T(8,128)S(1)}, f32[16,1024]{1,0:T(8,128)}, u32[]{:S(2)}) copy-start(f32[16,1024]{1,0:T(8,128)} %param.13) | copy-start | bytes 196612
  135.6 15.4 %all-to-all-start.1 = ((f32[8,16,1024]{2,1,0:T(8,128)}), f32[8,16,1024]{2,1,0:T(8,128)S(1)}, u32[]{:S(2)}, u32[]{:S(2)}) async-start(f32[8,16,1024]{2,1,0:T(8,128)} %broadcast_in_dim.24), calls=%async_computation.1 | async-start | bytes 1048576 | tf_op jit(solution)/shard_map/all_to_all | solution.py:56
  161.4 6.9 %copy-start.5 = (bf16[16,1024]{1,0:T(8,128)(2,1)S(1)}, bf16[16,1024]{1,0:T(8,128)(2,1)}, u32[]{:S(2)}) copy-start(bf16[16,1024]{1,0:T(8,128)(2,1)} %param.15) | copy-start | bytes 98308
  161.4 142.0 %all-to-all-start.2 = ((bf16[64,17,1024]{2,1,0:T(8,128)(2,1)}), bf16[64,17,1024]{2,1,0:T(8,128)(2,1)}, u32[]{:S(2)}, u32[]{:S(2)}) async-start(bf16[64,17,1024]{2,1,0:T(8,128)(2,1)} %broadcast_in_dim.25), calls=%async_computation.2 | async-start | bytes 6291456 | tf_op jit(solution)/shard_map/all_to_all | solution.py:65
  168.2 132.0 %all-gather.2.cloned.1.call-start = ((), (), s32[]{:S(2)}) async-start(), calls=%async_computation.5 | async-start | bytes 2359296 | tf_op jit(solution)/shard_map/all_gather | solution.py:30
  303.4 1.9 copy-start.4
  305.3 31.6 %copy-start.3 = (f32[16,1024]{1,0:T(8,128)S(1)}, f32[16,1024]{1,0:T(8,128)}, u32[]{:S(2)}) copy-start(f32[16,1024]{1,0:T(8,128)} %param.12) | copy-start | bytes 196612
  309.5 26.0 %all-to-all-start.3 = ((f32[64,1,128]{2,1,0:T(1,128)}), f32[64,1,128]{2,1,0:T(1,128)S(1)}, u32[]{:S(2)}, u32[]{:S(2)}) async-start(f32[64,1,128]{2,1,0:T(1,128)} %broadcast_in_dim.26), calls=%async_computation.3 | async-start | bytes 65536 | tf_op jit(solution)/shard_map/all_to_all | solution.py:72
  339.2 5.7 %copy-start.6 = (s32[128]{0:T(128)S(1)}, s32[128]{0:T(128)}, u32[]{:S(2)}) copy-start(s32[128]{0:T(128)} %param.17) | copy-start | bytes 1540
  339.2 58.5 %all-to-all-start.4 = ((bf16[64,16,1024]{2,1,0:T(8,128)(2,1)}), bf16[64,16,1024]{2,1,0:T(8,128)(2,1)}, u32[]{:S(2)}, u32[]{:S(2)}) async-start(bf16[64,16,1024]{2,1,0:T(8,128)(2,1)} %broadcast_in_dim.53), calls=%async_computation.4 | async-start | bytes 4194304 | tf_op jit(solution)/shard_map/all_to_all | solution.py:76
  353.7 1.3 copy-start.1
Sparse Core Ops, SparseCore 0:
  241.4 58.7 all-gather.1

commit v3 on v2

--- a/solution.py
+++ b/solution.py
@@ -43,7 +43,6 @@
     owner_index = lax.axis_index(OWN)
     grp_size = SUB_SIZES[0] * SUB_SIZES[1]
 
-    right_full = gather_own_rows(right_root)
 
     partial = lax.dot_general(
         activations, out_grads, (((0,), (0,)), ((), ())), preferred_element_type=jnp.float32
@@ -60,11 +59,14 @@
     adam_part = split3(jnp.sum(adam_dir * adam_dir))
 
     extra = jnp.zeros((1, block_size), jnp.float32).at[0, :3].set(adam_part)
-    payload = jnp.concatenate([grad_rows, extra], axis=0).astype(jnp.bfloat16)
+    payload = jnp.concatenate(
+        [grad_rows.astype(jnp.bfloat16), extra.astype(jnp.bfloat16), right_root], axis=0
+    )
     sent = jnp.broadcast_to(payload[None], (owners,) + payload.shape)
     got = lax.all_to_all(sent, OWN, 0, 0, tiled=True)
     grad_low = got[:, :owner_rows, :].reshape(block_size, block_size)
     adam_sum = jnp.sum(got[:, owner_rows, :3].astype(jnp.float32))
+    right_full = got[:, owner_rows + 1 :, :].reshape(block_size, block_size)
 
     left_mid = jnp.dot(left_root, grad_low, preferred_element_type=jnp.float32).astype(jnp.bfloat16)
     precond = jnp.dot(left_mid, right_full, preferred_element_type=jnp.float32)

time: 409 us -> 380 us (0.929)
  the two profiles are of different devices: /device:TPU:8 before, /device:TPU:1 now
where the time goes in v3:
time: 380 us; the launch traced here: 377 us
  blocking collectives  237 us (62%)
  waiting for transfers between devices  65.8 us (17%)
  starting transfers between devices  30.8 us (8%)
  between operations  13.9 us (4%)
  local copies, waits for them, and re-layouts  12.7 us (3%)
  other arithmetic  10.5 us (3%)
  matrix products  6.56 us (2%)
    all_to_all x1, blocking collectives, local(): got = lax.all_to_all(sent, OWN, 0, 0, tiled=True)  127 us
    all_to_all x1, blocking collectives, local(): lax.all_to_all(partial.reshape(owners, owner_rows, block_size), OWN, 0, 0...  110 us
    all_to_all x1, waiting for transfers between devices, local(): lax.all_to_all(weight_rows, OWN, 0, 0, tiled=True)  41.3 us
    all_to_all x1, starting transfers between devices, local(): grad_rows = jnp.sum(lax.all_to_all(copies, GRP, 0, 0, tiled=True), axis=0)  17.1 us
    all_to_all x1, waiting for transfers between devices, local(): grad_rows = jnp.sum(lax.all_to_all(copies, GRP, 0, 0, tiled=True), axis=0)  13.7 us
    all_to_all x1, waiting for transfers between devices, local(): lax.all_to_all(precond_part, OWN, 0, 0, tiled=True)[:, 0, 0]  10.8 us
    all_to_all x1, starting transfers between devices, local(): lax.all_to_all(precond_part, OWN, 0, 0, tiled=True)[:, 0, 0]  7.99 us
  transfers between devices with their start and end apart: 3, of which 3 were waited for; matrix products, arithmetic and copies ran while one was open for 2% of the time, Pallas kernels for 0%

profile of v3, /device:TPU:1, one launch (start us, length us, event | category | flops | bytes accessed | tf_op | source)
XLA Modules:
  0.0 377.5 jit_solution(2002554775119616099)
XLA Ops:
  0.6 0.0 copy-start
  0.6 0.9 copy-done
  1.6 1.7 fusion.17
  3.3 109.8 %all_to_all.25 = f32[64,16,1024]{2,1,0:T(8,128)} all-to-all(f32[64,16,1024]{2,1,0:T(8,128)S(1)} %bitcast.37), channel_id=1, replica_groups=mesh['yl'=4,'c'=2,'x'=4,'yh'=2,'z'=8] {'x','yh','z'}, dimensions={0} | all-to-all | bytes 8388608 | tf_op jit(solution)/shard_map/all_to_all | solution.py:50
  113.1 2.4 reduce_sum.72
  115.5 0.0 copy-start.3
  115.5 0.0 copy-start.6
  115.5 0.8 broadcast_in_dim.24
  116.4 17.1 %all-to-all-start.1 = ((f32[8,16,1024]{2,1,0:T(8,128)}), f32[8,16,1024]{2,1,0:T(8,128)S(1)}, u32[]{:S(2)}, u32[]{:S(2)}) async-start(f32[8,16,1024]{2,1,0:T(8,128)} %broadcast_in_dim.24), calls=%async_computation.1 | async-start | bytes 1048576 | tf_op jit(solution)/shard_map/all_to_all | solution.py:55
  133.4 0.6 compare_reduce_fusion
  134.1 13.7 %all-to-all-done.1 = f32[8,16,1024]{2,1,0:T(8,128)S(1)} async-done(((f32[8,16,1024]{2,1,0:T(8,128)}), f32[8,16,1024]{2,1,0:T(8,128)S(1)}, u32[]{:S(2)}, u32[]{:S(2)}) %all-to-all-start.1) | async-done | bytes 524320 | tf_op jit(solution)/shard_map/all_to_all | solution.py:55
  147.8 0.0 copy-done.3
  147.8 1.3 multiply_reduce_fusion.1
  153.3 2.7 fusion.12
  156.0 0.0 copy-done.6
  156.0 0.7 broadcast_in_dim.25
  156.7 127.4 %all_to_all.26 = bf16[64,33,1024]{2,1,0:T(8,128)(2,1)S(1)} all-to-all(bf16[64,33,1024]{2,1,0:T(8,128)(2,1)S(1)} %broadcast_in_dim.25), channel_id=1, replica_groups=mesh['yl'=4,'c'=2,'x'=4,'yh'=2,'z'=8] {'x','yh','z'}, dimensions={0} | all-to-all | bytes 8650752 | tf_op jit(solution)/shard_map/all_to_all | solution.py:66
  284.1 0.0 copy-start.1
  284.1 0.0 copy-start.5
  284.1 3.0 fusion.15
  287.1 0.0 copy-done.1
  287.1 0.0 copy-done.5
  287.1 0.0 copy-start.4
  287.1 2.9 multiply_reduce_fusion
  290.0 1.3 broadcast_in_dim.26
  291.3 8.0 %all-to-all-start.3 = ((f32[64,1,128]{2,1,0:T(1,128)}), f32[64,1,128]{2,1,0:T(1,128)S(1)}, u32[]{:S(2)}, u32[]{:S(2)}) async-start(f32[64,1,128]{2,1,0:T(1,128)} %broadcast_in_dim.26), calls=%async_computation.3 | async-start | bytes 65536 | tf_op jit(solution)/shard_map/all_to_all | solution.py:74
  299.3 1.6 fusion.9
  301.6 10.8 %all-to-all-done.3 = f32[64,1,128]{2,1,0:T(1,128)S(1)} async-done(((f32[64,1,128]{2,1,0:T(1,128)}), f32[64,1,128]{2,1,0:T(1,128)S(1)}, u32[]{:S(2)}, u32[]{:S(2)}) %all-to-all-start.3) | async-done | bytes 32800 | tf_op jit(solution)/shard_map/all_to_all | solution.py:74
  312.4 0.7 slice_reduce_fusion
  313.8 0.0 copy-done.4
  313.8 0.6 fusion.13
  314.4 1.6 broadcast_in_dim.53
  316.0 0.0 copy-start.7
  316.0 5.7 %all-to-all-start.4 = ((bf16[64,16,1024]{2,1,0:T(8,128)(2,1)}), bf16[64,16,1024]{2,1,0:T(8,128)(2,1)}, u32[]{:S(2)}, u32[]{:S(2)}) async-start(bf16[64,16,1024]{2,1,0:T(8,128)(2,1)} %broadcast_in_dim.53), calls=%async_computation.4 | async-start | bytes 4194304 | tf_op jit(solution)/shard_map/all_to_all | solution.py:78
  321.7 0.0 copy-done.7
  321.8 0.2 fusion.10
  322.0 0.6 fusion.16
  330.1 0.5 dynamic-slice_bitcast_fusion.3
  330.6 0.0 copy-start.2
  330.6 0.4 pad_maximum_fusion
  330.9 0.1 copy.16
  331.1 0.1 constant_dynamic-slice_fusion.3
  331.1 0.8 fusion.18
  331.9 0.0 copy-done.2
  331.9 1.2 fusion.2
  333.1 41.3 %all-to-all-done.4 = bf16[64,16,1024]{2,1,0:T(8,128)(2,1)} async-done(((bf16[64,16,1024]{2,1,0:T(8,128)(2,1)}), bf16[64,16,1024]{2,1,0:T(8,128)(2,1)}, u32[]{:S(2)}, u32[]{:S(2)}) %all-to-all-start.4) | async-done | bytes 2097184 | tf_op jit(solution)/shard_map/all_to_all | solution.py:78
  374.4 3.1 copy.19
  (7 shorter events, 0.1 us)
Async XLA Ops:
  0.6 1.0 copy-start
  115.5 32.3 %copy-start.3 = (f32[16,1024]{1,0:T(8,128)S(1)}, f32[16,1024]{1,0:T(8,128)}, u32[]{:S(2)}) copy-start(f32[16,1024]{1,0:T(8,128)} %param.13) | copy-start | bytes 196612
  115.5 40.5 %copy-start.6 = (bf16[16,1024]{1,0:T(8,128)(2,1)S(1)}, bf16[16,1024]{1,0:T(8,128)(2,1)}, u32[]{:S(2)}) copy-start(bf16[16,1024]{1,0:T(8,128)(2,1)} %param.15) | copy-start | bytes 98308
  116.4 31.4 %all-to-all-start.1 = ((f32[8,16,1024]{2,1,0:T(8,128)}), f32[8,16,1024]{2,1,0:T(8,128)S(1)}, u32[]{:S(2)}, u32[]{:S(2)}) async-start(f32[8,16,1024]{2,1,0:T(8,128)} %broadcast_in_dim.24), calls=%async_computation.1 | async-start | bytes 1048576 | tf_op jit(solution)/shard_map/all_to_all | solution.py:55
  284.1 3.0 copy-start.1
  284.1 3.0 copy-start.5
  287.1 26.7 %copy-start.4 = (f32[16,1024]{1,0:T(8,128)S(1)}, f32[16,1024]{1,0:T(8,128)}, u32[]{:S(2)}) copy-start(f32[16,1024]{1,0:T(8,128)} %param.12) | copy-start | bytes 196612
  291.3 21.1 %all-to-all-start.3 = ((f32[64,1,128]{2,1,0:T(1,128)}), f32[64,1,128]{2,1,0:T(1,128)S(1)}, u32[]{:S(2)}, u32[]{:S(2)}) async-start(f32[64,1,128]{2,1,0:T(1,128)} %broadcast_in_dim.26), calls=%async_computation.3 | async-start | bytes 65536 | tf_op jit(solution)/shard_map/all_to_all | solution.py:74
  316.0 5.7 %copy-start.7 = (s32[128]{0:T(128)S(1)}, s32[128]{0:T(128)}, u32[]{:S(2)}) copy-start(s32[128]{0:T(128)} %param.17) | copy-start | bytes 1540
  316.0 58.4 %all-to-all-start.4 = ((bf16[64,16,1024]{2,1,0:T(8,128)(2,1)}), bf16[64,16,1024]{2,1,0:T(8,128)(2,1)}, u32[]{:S(2)}, u32[]{:S(2)}) async-start(bf16[64,16,1024]{2,1,0:T(8,128)(2,1)} %broadcast_in_dim.53), calls=%async_computation.4 | async-start | bytes 4194304 | tf_op jit(solution)/shard_map/all_to_all | solution.py:78
  330.6 1.3 copy-start.2
